TPU v7x, 512 devices: a whole 4x8x8 slice. The times are simulated.
512 devices in a mesh: req: 64 (over z, x, core), tp: 8 (over y).
Axes of the slice: x: 4, y: 8, z: 8, core: 2. Of those that a mesh axis runs over, the one named last changes fastest.
Arguments:
- queries: bfloat16 [16384, 7168], P('req', 'tp'), may hold values from -200 to 200
- key_value: bfloat16 [2, 16384, 1024], P(None, 'req', 'tp'), may hold values from -8 to 8
- segment: int32 [16384], P('req'), may hold values from 0 to 31, never falling along the last dimension, each value on 1 to 1024 neighbouring positions
- residual: bfloat16 [16384, 7168], P('req', 'tp'), may hold values from -4 to 4
- out_weight: bfloat16 [7168, 7168], P('tp', 'req'), may hold values from -0.0625 to 0.0625
- head_gain: bfloat16 [7168], P('tp'), may hold values from 0.099609375 to 1.8984375
- vocab_weight: bfloat16 [7168, 64000], P('tp', 'req'), may hold values from -0.21875 to 0.21875
Outputs:
- hidden: bfloat16 [16384, 7168], P('req', 'tp')
- key_cache: bfloat16 [16384, 1024], P('req', 'tp')
- last_norm: float32 [32], replicated
- top_logit: float32 [32], replicated
Inputs may be any that keep to these rules, and one draw needn't show every extreme that they name: `segment`: ids never fall; each of the 32 requests has 1 to 1024 tokens, one has exactly 1024.
All inputs are finite; a program needn't handle non-finite values.
Results may differ from a plain program's by a relative error of at most 0.013.
Values may be sent and summed in bfloat16 or wider, within the bound.
No kernel may reach another device: no remote copies, remote signals or barrier semaphores. Data moves between devices by JAX's collectives and lax.ppermute only.
A program may use at most 128 MiB of HBM per device.

v0:
```python
import jax
import jax.numpy as jnp
from jax import lax
from jax.sharding import PartitionSpec as P

D = 7168
HD = 128
GROUP = 7
REACH = 4
theta = 5000000.0
eps = 1e-05
masked_score = -1e30


def from_behind(value, axis, steps):
    count = lax.axis_size(axis)
    initial, last = (max(0, -steps), min(count, count - steps))
    return lax.ppermute(value, axis, [(source, source + steps) for source in range(initial, last)])


def butterfly(value, axis, combine):
    count = lax.axis_size(axis)
    stride = 1
    while stride < count:
        other = lax.ppermute(value, axis, [(source, source ^ stride) for source in range(count)])
        value = combine(value, other)
        stride *= 2
    return value


def halving_scatter(value, axis):
    count = lax.axis_size(axis)
    index = lax.axis_index(axis)
    rows, width = (value.shape[1], value.shape[2])
    held = jnp.moveaxis(value, 0, 1)
    bit = 1
    while bit < count:
        mine = index // bit % 2
        pairs = held.reshape(rows, held.shape[1] // 2, 2, width)
        keep = lax.dynamic_index_in_dim(pairs, mine, 2, keepdims=False)
        give = lax.dynamic_index_in_dim(pairs, 1 - mine, 2, keepdims=False)
        moved = lax.ppermute(give, axis, [(source, source ^ bit) for source in range(count)])
        held = (keep.astype(jnp.float32) + moved.astype(jnp.float32)).astype(value.dtype)
        bit *= 2
    return held.reshape(rows, width).astype(jnp.float32)


def rope_tables(positions, width):
    half_width = width // 2
    frequency = theta ** (-(jnp.arange(half_width, dtype=jnp.float32) * 2.0 / width))
    angles = positions[:, None] * frequency[None, :]
    return (jnp.cos(angles), jnp.sin(angles))


def rotate(values, cosine, sine_table):
    half_width = values.shape[-1] // 2
    first_half = values[..., :half_width]
    second_half = values[..., half_width:]
    table_shape = (cosine.shape[0],) + (1,) * (values.ndim - 2) + (half_width,)
    cosine = cosine.reshape(table_shape)
    sine_table = sine_table.reshape(table_shape)
    return jnp.concatenate(
        [
            first_half * cosine - second_half * sine_table,
            second_half * cosine + first_half * sine_table,
        ],
        axis=-1,
    )


def local(queries, key_value, segment, residual, out_weight, head_gain, vocab_weight):
    tok_rows = segment.shape[0]
    heads_kv = key_value.shape[2] // HD
    requests = lax.axis_size("req") // 2
    devices_req = lax.axis_size("req")
    device = lax.axis_index("req")
    request_ids = jnp.arange(requests, dtype=jnp.int32)
    own_kv = key_value
    width = own_kv.shape[2]
    seg_rows = -(-tok_rows // width)
    seg_flat = jnp.pad(segment, (0, seg_rows * width - tok_rows)).astype(jnp.bfloat16)
    packed = jnp.concatenate(
        [own_kv.reshape(2 * tok_rows, width), seg_flat.reshape(seg_rows, width)], axis=0
    )
    parts_kv, parts_seg = ([], [])
    for back in range(REACH, 0, -1):
        got = from_behind(packed, "req", back)
        parts_kv.append(got[: 2 * tok_rows].reshape(own_kv.shape))
        parts_seg.append(got[2 * tok_rows :].reshape(-1)[:tok_rows].astype(jnp.int32))
    parts_kv.append(own_kv)
    parts_seg.append(segment)
    window = jnp.concatenate(parts_kv, axis=1)
    seg_window = jnp.concatenate(parts_seg, axis=0)
    span = window.shape[1]
    key_index_i = (device - REACH) * tok_rows + jnp.arange(span, dtype=jnp.int32)
    valid = key_index_i >= 0
    same = (seg_window[:, None] == seg_window[None, :]) & valid[None, :]
    start_i = jnp.min(jnp.where(same, key_index_i[None, :], jnp.int32(2**30)), axis=1)
    key_index = key_index_i.astype(jnp.float32)
    win_start = start_i.astype(jnp.float32)
    win_pos = key_index - win_start
    own_start = win_start[span - tok_rows :]
    tok_index = key_index[span - tok_rows :]
    positions = win_pos[span - tok_rows :]
    cosine, sine_table = rope_tables(win_pos, HD)
    rot_keys = rotate(
        window[0].astype(jnp.float32).reshape(span, heads_kv, HD), cosine, sine_table
    ).astype(jnp.bfloat16)
    q_cos, q_sin = (cosine[span - tok_rows :], sine_table[span - tok_rows :])
    rot_query = rotate(
        queries.astype(jnp.float32).reshape(tok_rows, heads_kv, GROUP, HD), q_cos, q_sin
    ).astype(jnp.bfloat16)
    key_cache = rot_keys[span - tok_rows :].reshape(tok_rows, heads_kv * HD)
    key_rows = rot_keys
    value_rows = window[1].reshape(span, heads_kv, HD)
    q_seg = segment
    allowed = (
        (seg_window[None, :] == q_seg[:, None])
        & valid[None, :]
        & (key_index[None, :] <= tok_index[:, None])
    )
    scale = HD ** (-0.5)
    scores_part = (
        jnp.einsum("qhgd,khd->hgqk", rot_query, key_rows, preferred_element_type=jnp.float32)
        * scale
    )
    scores = jnp.where(allowed[None, None], scores_part, masked_score)
    peak = jnp.max(scores, axis=3, keepdims=True)
    weights = jnp.exp(scores - peak)
    total = jnp.sum(weights, axis=3)
    context = jnp.einsum(
        "hgqk,khd->qhgd",
        weights.astype(jnp.bfloat16),
        value_rows,
        preferred_element_type=jnp.float32,
    )
    context = context / jnp.transpose(total, (2, 0, 1))[..., None]
    attended = context.astype(jnp.bfloat16).reshape(tok_rows, heads_kv * GROUP * HD)
    is_end = jnp.concatenate([segment[1:] != segment[:-1], jnp.ones((1,), bool)])
    select = (is_end[:, None] & (segment[:, None] == request_ids[None, :])).astype(jnp.bfloat16)
    held = jnp.any(segment[:, None] == request_ids[None, :], axis=0)
    tag = jnp.where(held, device, -1).astype(jnp.bfloat16)
    end_rows = lax.dot_general(
        select,
        jnp.concatenate([attended, residual], axis=1),
        (((0,), (0,)), ((), ())),
        preferred_element_type=jnp.float32,
    ).astype(jnp.bfloat16)
    end_rows = jnp.concatenate([end_rows, tag[:, None]], axis=1)

    def latest(mine, other):
        return jnp.where(other[:, -1:] > mine[:, -1:], other, mine)

    end_rows = butterfly(end_rows, "req", latest)[:, :-1]
    attended, end_rows = lax.optimization_barrier((attended, end_rows))
    end_att, end_res = (end_rows[:, : attended.shape[1]], end_rows[:, attended.shape[1] :])
    full_weight = lax.all_gather(out_weight, "req", axis=1, tiled=True)
    groups = lax.axis_size("tp")
    both = jnp.einsum(
        "tk,kgn->gtn",
        jnp.concatenate([attended, end_att], axis=0),
        full_weight.reshape(full_weight.shape[0], groups, -1),
        preferred_element_type=jnp.float32,
    ).astype(jnp.bfloat16)
    end_part = both[:, tok_rows:]
    end_sum = halving_scatter(end_part, "tp")
    both, end_sum = lax.optimization_barrier((both, end_sum))
    own_share = lax.psum_scatter(both, "tp", scatter_dimension=0, tiled=True)[0, :tok_rows]
    own_share = own_share.astype(jnp.float32)
    hidden = (residual.astype(jnp.float32) + own_share).astype(jnp.bfloat16)
    last_state = (end_res.astype(jnp.float32) + end_sum).astype(jnp.bfloat16).astype(jnp.float32)
    scaled = (last_state * head_gain.astype(jnp.float32)).astype(jnp.bfloat16)
    square_part = jnp.sum(last_state * last_state, axis=1)
    logit_part = jnp.dot(scaled, vocab_weight, preferred_element_type=jnp.float32)
    summed = butterfly(
        jnp.concatenate([logit_part, square_part[:, None]], axis=1).astype(jnp.bfloat16),
        "tp",
        jnp.add,
    ).astype(jnp.float32)
    raw_logits, square_sum = (summed[:, :-1], summed[:, -1])
    mean_square = square_sum / D
    last_norm = jnp.sqrt(mean_square)
    local_top = jnp.max(raw_logits * lax.rsqrt(mean_square + eps)[:, None], axis=1)
    top_logit = butterfly(local_top, "req", jnp.maximum)
    return (hidden, key_cache, last_norm, top_logit)


def solution(mesh):
    placed = (
        P("req", "tp"),
        P(None, "req", "tp"),
        P("req"),
        P("req", "tp"),
        P("tp", "req"),
        P("tp"),
        P("tp", "req"),
    )
    return jax.shard_map(
        local,
        mesh=mesh,
        in_specs=placed,
        out_specs=(P("req", "tp"), P("req", "tp"), P(), P()),
        check_vma=False,
    )
```

profile of v0, /device:TPU:56, one launch (start us, length us, event | category | flops | bytes accessed | tf_op | source)
XLA Modules:
  0.0 238.6 jit_solution(11665168954545086751)
XLA Ops:
  9.6 4.9 %collective-permute-start = (bf16[514,128]{1,0:T(8,128)(2,1)S(1)}, bf16[514,128]{1,0:T(8,128)(2,1)S(1)}, u32[]{:S(2)}, u32[]{:S(2)}) collective-permute-start(bf16[514,128]{1,0:T(8,128)(2,1)S(1)} %pad_maximum_fusion), channel_id=1, source_target_pairs={{0,32},{8,40},{16,48},{24,56},{32,64},{40,72},{48,80},{56,88},{64,... | collective-permute-start | bytes 394760 | tf_op jit(solution)/shard_map/ppermute | solution.py:18
  16.8 4.2 %collective-permute-start.2 = (bf16[514,128]{1,0:T(8,128)(2,1)S(1)}, bf16[514,128]{1,0:T(8,128)(2,1)}, u32[]{:S(2)}, u32[]{:S(2)}) collective-permute-start(bf16[514,128]{1,0:T(8,128)(2,1)S(1)} %pad_maximum_fusion), channel_id=1, source_target_pairs={{0,16},{8,24},{16,32},{24,40},{32,48},{40,56},{48,64},{56,72},{64,... | collective-permute-start | bytes 394760 | tf_op jit(solution)/shard_map/ppermute | solution.py:18
  21.1 4.1 %collective-permute-start.3 = (bf16[514,128]{1,0:T(8,128)(2,1)S(1)}, bf16[514,128]{1,0:T(8,128)(2,1)}, u32[]{:S(2)}, u32[]{:S(2)}) collective-permute-start(bf16[514,128]{1,0:T(8,128)(2,1)S(1)} %pad_maximum_fusion), channel_id=1, source_target_pairs={{0,8},{8,16},{16,24},{24,32},{32,40},{40,48},{48,56},{56,64},{64,7... | collective-permute-start | bytes 394760 | tf_op jit(solution)/shard_map/ppermute | solution.py:18
  43.3 3.0 %fusion.25 = (bf16[1280,1,64]{2,0,1:T(8,128)(2,1)S(1)}, bf16[1280,1,64]{2,0,1:T(8,128)(2,1)S(1)}) fusion(f32[1280,1,128]{2,0,1:T(8,128)S(1)} %fusion.37, f32[64]{0:T(128)S(1)} %negate_power_fusion, f32[1280]{0:T(1024)S(1)} %convert_subtract_fusion), kind=kLoop, calls=%fused_computation.30 | loop fusion | flops 737280 | bytes 988416 | tf_op jit(solution)/shard_map/convert.22
  60.0 4.9 %collective-permute-done.5 = bf16[32,1793]{1,0:T(8,128)(2,1)S(1)} collective-permute-done((bf16[32,1793]{1,0:T(8,128)(2,1)S(1)}, bf16[32,1793]{1,0:T(8,128)(2,1)S(1)}, u32[]{:S(2)}, u32[]{:S(2)}) %collective-permute-start.5) | collective-permute-done | bytes 114784 | tf_op jit(solution)/shard_map/ppermute | solution.py:25
  65.1 4.1 %collective-permute-start.6 = (bf16[32,1793]{1,0:T(8,128)(2,1)S(1)}, bf16[32,1793]{1,0:T(8,128)(2,1)S(1)}, u32[]{:S(2)}, u32[]{:S(2)}) collective-permute-start(bf16[32,1793]{1,0:T(8,128)(2,1)S(1)} %broadcast_select_fusion.3), channel_id=1, source_target_pairs={{0,32},{8,40},{16,48},{24,56},{32,0},{40,8},{48,16},{56,24},{64,96... | collective-permute-start | bytes 344264 | tf_op jit(solution)/shard_map/ppermute | solution.py:25
  69.2 4.2 %collective-permute-done.6 = bf16[32,1793]{1,0:T(8,128)(2,1)S(1)} collective-permute-done((bf16[32,1793]{1,0:T(8,128)(2,1)S(1)}, bf16[32,1793]{1,0:T(8,128)(2,1)S(1)}, u32[]{:S(2)}, u32[]{:S(2)}) %collective-permute-start.6) | collective-permute-done | bytes 114784 | tf_op jit(solution)/shard_map/ppermute | solution.py:25
  73.6 4.6 %collective-permute-start.7 = (bf16[32,1793]{1,0:T(8,128)(2,1)S(1)}, bf16[32,1793]{1,0:T(8,128)(2,1)S(1)}, u32[]{:S(2)}, u32[]{:S(2)}) collective-permute-start(bf16[32,1793]{1,0:T(8,128)(2,1)S(1)} %broadcast_select_fusion.2), channel_id=1, source_target_pairs={{0,64},{8,72},{16,80},{24,88},{32,96},{40,104},{48,112},{56,120},{... | collective-permute-start | bytes 344264 | tf_op jit(solution)/shard_map/ppermute | solution.py:25
  78.2 5.2 %collective-permute-done.7 = bf16[32,1793]{1,0:T(8,128)(2,1)S(1)} collective-permute-done((bf16[32,1793]{1,0:T(8,128)(2,1)S(1)}, bf16[32,1793]{1,0:T(8,128)(2,1)S(1)}, u32[]{:S(2)}, u32[]{:S(2)}) %collective-permute-start.7) | collective-permute-done | bytes 114784 | tf_op jit(solution)/shard_map/ppermute | solution.py:25
  83.6 7.3 %collective-permute-start.8 = (bf16[32,1793]{1,0:T(8,128)(2,1)S(1)}, bf16[32,1793]{1,0:T(8,128)(2,1)S(1)}, u32[]{:S(2)}, u32[]{:S(2)}) collective-permute-start(bf16[32,1793]{1,0:T(8,128)(2,1)S(1)} %broadcast_select_fusion.1), channel_id=1, source_target_pairs={{0,128},{8,136},{16,144},{24,152},{32,160},{40,168},{48,176},{56,1... | collective-permute-start | bytes 344264 | tf_op jit(solution)/shard_map/ppermute | solution.py:25
  90.9 7.8 %collective-permute-done.8 = bf16[32,1793]{1,0:T(8,128)(2,1)S(1)} collective-permute-done((bf16[32,1793]{1,0:T(8,128)(2,1)S(1)}, bf16[32,1793]{1,0:T(8,128)(2,1)S(1)}, u32[]{:S(2)}, u32[]{:S(2)}) %collective-permute-start.8) | collective-permute-done | bytes 114784 | tf_op jit(solution)/shard_map/ppermute | solution.py:25
  98.9 6.5 %collective-permute-start.9 = (bf16[32,1793]{1,0:T(8,128)(2,1)S(1)}, bf16[32,1793]{1,0:T(8,128)(2,1)S(1)}, u32[]{:S(2)}, u32[]{:S(2)}) collective-permute-start(bf16[32,1793]{1,0:T(8,128)(2,1)S(1)} %broadcast_select_fusion), channel_id=1, source_target_pairs={{0,256},{8,264},{16,272},{24,280},{32,288},{40,296},{48,304},{56,3... | collective-permute-start | bytes 344264 | tf_op jit(solution)/shard_map/ppermute | solution.py:25
  105.4 8.2 %collective-permute-done.9 = bf16[32,1793]{1,0:T(8,128)(2,1)S(1)} collective-permute-done((bf16[32,1793]{1,0:T(8,128)(2,1)S(1)}, bf16[32,1793]{1,0:T(8,128)(2,1)S(1)}, u32[]{:S(2)}, u32[]{:S(2)}) %collective-permute-start.9) | collective-permute-done | bytes 114784 | tf_op jit(solution)/shard_map/ppermute | solution.py:25
  114.8 7.7 %all-gather.2.cloned.1.call-done = bf16[896,7168]{0,1:T(8,128)(2,1)} async-done(((bf16[896,112]{0,1:T(8,128)(2,1)}), bf16[896,7168]{0,1:T(8,128)(2,1)}) %all-gather.2.cloned.1.call-update) | async-done | bytes 12845072 | tf_op jit(solution)/shard_map/all_gather | solution.py:157
  122.5 11.2 %convert_bitcast_fusion = bf16[8,288,896]{2,1,0:T(8,128)(2,1)} fusion(bf16[896,8,896]{0,2,1:T(8,128)(2,1)} %bitcast.151, bf16[32,896]{1,0:T(8,128)(2,1)S(1)} %slice.145, bf16[256,896]{1,0:T(8,128)(2,1)} %copy.39), kind=kOutput, calls=%fused_computation.9 | convolution fusion | flops 3702472704 | bytes 17489920 | tf_op jit(solution)/shard_map/tk,kgn->gtn/dot_general | solution.py:159
  134.8 3.2 %collective-permute-start.10 = (bf16[32,4,896]{2,0,1:T(8,128)(2,1)S(1)}, bf16[32,4,896]{2,0,1:T(8,128)(2,1)S(1)}, u32[]{:S(2)}, u32[]{:S(2)}) collective-permute-start(bf16[32,4,896]{2,0,1:T(8,128)(2,1)S(1)} %dynamic-slice_bitcast_fusion), channel_id=1, source_target_pairs={{0,1},{1,0},{2,3},{3,2},{4,5},{5,4},{6,7},{7,6},{8,9},{9,8},{10,11... | collective-permute-start | bytes 688136 | tf_op jit(solution)/shard_map/ppermute | solution.py:42
  138.0 6.4 %collective-permute-done.10 = bf16[32,4,896]{2,0,1:T(8,128)(2,1)S(1)} collective-permute-done((bf16[32,4,896]{2,0,1:T(8,128)(2,1)S(1)}, bf16[32,4,896]{2,0,1:T(8,128)(2,1)S(1)}, u32[]{:S(2)}, u32[]{:S(2)}) %collective-permute-start.10) | collective-permute-done | bytes 229408 | tf_op jit(solution)/shard_map/ppermute | solution.py:42
  144.5 3.9 %collective-permute-start.11 = (bf16[32,2,896]{2,0,1:T(8,128)(2,1)S(1)}, bf16[32,2,896]{2,0,1:T(8,128)(2,1)S(1)}, u32[]{:S(2)}, u32[]{:S(2)}) collective-permute-start(bf16[32,2,896]{2,0,1:T(8,128)(2,1)S(1)} %dynamic-slice_bitcast_fusion.1), channel_id=1, source_target_pairs={{0,2},{1,3},{2,0},{3,1},{4,6},{5,7},{6,4},{7,5},{8,10},{9,11},{10,... | collective-permute-start | bytes 344072 | tf_op jit(solution)/shard_map/ppermute | solution.py:42
  148.5 5.8 %collective-permute-done.11 = bf16[32,2,896]{2,0,1:T(8,128)(2,1)S(1)} collective-permute-done((bf16[32,2,896]{2,0,1:T(8,128)(2,1)S(1)}, bf16[32,2,896]{2,0,1:T(8,128)(2,1)S(1)}, u32[]{:S(2)}, u32[]{:S(2)}) %collective-permute-start.11) | collective-permute-done | bytes 114720 | tf_op jit(solution)/shard_map/ppermute | solution.py:42
  154.3 4.1 %collective-permute-start.12 = (bf16[32,1,896]{2,0,1:T(8,128)(2,1)S(1)}, bf16[32,1,896]{2,0,1:T(8,128)(2,1)S(1)}, u32[]{:S(2)}, u32[]{:S(2)}) collective-permute-start(bf16[32,1,896]{2,0,1:T(8,128)(2,1)S(1)} %constant_dynamic-slice_fusion), channel_id=1, source_target_pairs={{0,4},{1,5},{2,6},{3,7},{4,0},{5,1},{6,2},{7,3},{8,12},{9,13},{10,... | collective-permute-start | bytes 172040 | tf_op jit(solution)/shard_map/ppermute | solution.py:42
  158.5 5.9 %collective-permute-done.12 = bf16[32,1,896]{2,0,1:T(8,128)(2,1)S(1)} collective-permute-done((bf16[32,1,896]{2,0,1:T(8,128)(2,1)S(1)}, bf16[32,1,896]{2,0,1:T(8,128)(2,1)S(1)}, u32[]{:S(2)}, u32[]{:S(2)}) %collective-permute-start.12) | collective-permute-done | bytes 57376 | tf_op jit(solution)/shard_map/ppermute | solution.py:42
  167.3 4.2 %collective-permute-done.13 = bf16[32,1001]{1,0:T(8,128)(2,1)S(1)} collective-permute-done((bf16[32,1001]{1,0:T(8,128)(2,1)S(1)}, bf16[32,1001]{1,0:T(8,128)(2,1)S(1)}, u32[]{:S(2)}, u32[]{:S(2)}) %collective-permute-start.13) | collective-permute-done | bytes 64096 | tf_op jit(solution)/shard_map/ppermute | solution.py:25
  171.6 3.3 %collective-permute-start.14 = (bf16[32,1001]{1,0:T(8,128)(2,1)S(1)}, bf16[32,1001]{1,0:T(8,128)(2,1)S(1)}, u32[]{:S(2)}, u32[]{:S(2)}) collective-permute-start(bf16[32,1001]{1,0:T(8,128)(2,1)S(1)} %fusion.64), channel_id=1, source_target_pairs={{0,2},{1,3},{2,0},{3,1},{4,6},{5,7},{6,4},{7,5},{8,10},{9,11},{10,... | collective-permute-start | bytes 192200 | tf_op jit(solution)/shard_map/ppermute | solution.py:25
  174.8 5.0 %collective-permute-done.14 = bf16[32,1001]{1,0:T(8,128)(2,1)S(1)} collective-permute-done((bf16[32,1001]{1,0:T(8,128)(2,1)S(1)}, bf16[32,1001]{1,0:T(8,128)(2,1)S(1)}, u32[]{:S(2)}, u32[]{:S(2)}) %collective-permute-start.14) | collective-permute-done | bytes 64096 | tf_op jit(solution)/shard_map/ppermute | solution.py:25
  179.8 4.4 %collective-permute-start.15 = (bf16[32,1001]{1,0:T(8,128)(2,1)S(1)}, bf16[32,1001]{1,0:T(8,128)(2,1)S(1)}, u32[]{:S(2)}, u32[]{:S(2)}) collective-permute-start(bf16[32,1001]{1,0:T(8,128)(2,1)S(1)} %add.116), channel_id=1, source_target_pairs={{0,4},{1,5},{2,6},{3,7},{4,0},{5,1},{6,2},{7,3},{8,12},{9,13},{10,... | collective-permute-start | bytes 192200 | tf_op jit(solution)/shard_map/ppermute | solution.py:25
  184.2 7.6 %collective-permute-done.15 = bf16[32,1001]{1,0:T(8,128)(2,1)S(1)} collective-permute-done((bf16[32,1001]{1,0:T(8,128)(2,1)S(1)}, bf16[32,1001]{1,0:T(8,128)(2,1)S(1)}, u32[]{:S(2)}, u32[]{:S(2)}) %collective-permute-start.15) | collective-permute-done | bytes 64096 | tf_op jit(solution)/shard_map/ppermute | solution.py:25
  201.2 3.2 %collective-permute-start.18 = (f32[32]{0:T(128)S(1)}, f32[32]{0:T(128)S(1)}, u32[]{:S(2)}, u32[]{:S(2)}) collective-permute-start(f32[32]{0:T(128)S(1)} %max.19), channel_id=1, source_target_pairs={{0,32},{8,40},{16,48},{24,56},{32,0},{40,8},{48,16},{56,24},{64,96... | collective-permute-start | bytes 392 | tf_op jit(solution)/shard_map/ppermute | solution.py:25
  204.4 3.7 %collective-permute-done.18 = f32[32]{0:T(128)S(1)} collective-permute-done((f32[32]{0:T(128)S(1)}, f32[32]{0:T(128)S(1)}, u32[]{:S(2)}, u32[]{:S(2)}) %collective-permute-start.18) | collective-permute-done | bytes 160 | tf_op jit(solution)/shard_map/ppermute | solution.py:25
  210.1 3.5 %collective-permute-done.19 = f32[32]{0:T(128)S(1)} collective-permute-done((f32[32]{0:T(128)S(1)}, f32[32]{0:T(128)S(1)}, u32[]{:S(2)}, u32[]{:S(2)}) %collective-permute-start.19) | collective-permute-done | bytes 160 | tf_op jit(solution)/shard_map/ppermute | solution.py:25
  215.6 4.3 %collective-permute-done.20 = f32[32]{0:T(128)S(1)} collective-permute-done((f32[32]{0:T(128)S(1)}, f32[32]{0:T(128)S(1)}, u32[]{:S(2)}, u32[]{:S(2)}) %collective-permute-start.20) | collective-permute-done | bytes 160 | tf_op jit(solution)/shard_map/ppermute | solution.py:25
  219.9 4.9 %collective-permute-start.21 = (f32[32]{0:T(128)S(1)}, f32[32]{0:T(128)S(1)}, u32[]{:S(2)}, u32[]{:S(2)}) collective-permute-start(f32[32]{0:T(128)S(1)} %max.22), channel_id=1, source_target_pairs={{0,256},{8,264},{16,272},{24,280},{32,288},{40,296},{48,304},{56,3... | collective-permute-start | bytes 392 | tf_op jit(solution)/shard_map/ppermute | solution.py:25
  225.6 3.7 %collective-permute-done.21 = f32[32]{0:T(128)S(1)} collective-permute-done((f32[32]{0:T(128)S(1)}, f32[32]{0:T(128)S(1)}, u32[]{:S(2)}, u32[]{:S(2)}) %collective-permute-start.21) | collective-permute-done | bytes 160 | tf_op jit(solution)/shard_map/ppermute | solution.py:25
  (108 shorter events, 59.0 us)
Async XLA Ops:
  7.2 157.4 %copy-start = (bf16[896,1000]{0,1:T(8,128)(2,1)S(1)}, bf16[896,1000]{0,1:T(8,128)(2,1)}, u32[]{:S(2)}) copy-start(bf16[896,1000]{0,1:T(8,128)(2,1)} %param.13) | copy-start | bytes 5376004
  7.2 35.0 %copy-start.1 = (s32[256]{0:T(256)S(1)}, s32[256]{0:T(256)}, u32[]{:S(2)}) copy-start(s32[256]{0:T(256)} %param.9) | copy-start | bytes 3076
  7.2 115.3 %all-gather.2.cloned.1.call-start = ((), (), s32[]{:S(2)}) async-start(), calls=%async_computation.1 | async-start | bytes 13045760 | tf_op jit(solution)/shard_map/all_gather | solution.py:157
  7.9 221.8 %reduce-scatter.2.cloned.1.call-start = ((), (), s32[]{:S(2)}) async-start(), calls=%async_computation.2 | async-start | bytes 4644864 | tf_op jit(solution)/shard_map/reduce_scatter | solution.py:168
  9.6 22.2 %collective-permute-start = (bf16[514,128]{1,0:T(8,128)(2,1)S(1)}, bf16[514,128]{1,0:T(8,128)(2,1)S(1)}, u32[]{:S(2)}, u32[]{:S(2)}) collective-permute-start(bf16[514,128]{1,0:T(8,128)(2,1)S(1)} %pad_maximum_fusion), channel_id=1, source_target_pairs={{0,32},{8,40},{16,48},{24,56},{32,64},{40,72},{48,80},{56,88},{64,... | collective-permute-start | bytes 394760 | tf_op jit(solution)/shard_map/ppermute | solution.py:18
  14.5 17.3 %collective-permute-start.1 = (bf16[514,128]{1,0:T(8,128)(2,1)S(1)}, bf16[514,128]{1,0:T(8,128)(2,1)}, u32[]{:S(2)}, u32[]{:S(2)}) collective-permute-start(bf16[514,128]{1,0:T(8,128)(2,1)S(1)} %pad_maximum_fusion), channel_id=1, source_target_pairs={{0,24},{8,32},{16,40},{24,48},{32,56},{40,64},{48,72},{56,80},{64,... | collective-permute-start | bytes 394760 | tf_op jit(solution)/shard_map/ppermute | solution.py:18
  16.8 15.9 %collective-permute-start.2 = (bf16[514,128]{1,0:T(8,128)(2,1)S(1)}, bf16[514,128]{1,0:T(8,128)(2,1)}, u32[]{:S(2)}, u32[]{:S(2)}) collective-permute-start(bf16[514,128]{1,0:T(8,128)(2,1)S(1)} %pad_maximum_fusion), channel_id=1, source_target_pairs={{0,16},{8,24},{16,32},{24,40},{32,48},{40,56},{48,64},{56,72},{64,... | collective-permute-start | bytes 394760 | tf_op jit(solution)/shard_map/ppermute | solution.py:18
  21.1 12.6 %collective-permute-start.3 = (bf16[514,128]{1,0:T(8,128)(2,1)S(1)}, bf16[514,128]{1,0:T(8,128)(2,1)}, u32[]{:S(2)}, u32[]{:S(2)}) collective-permute-start(bf16[514,128]{1,0:T(8,128)(2,1)S(1)} %pad_maximum_fusion), channel_id=1, source_target_pairs={{0,8},{8,16},{16,24},{24,32},{32,40},{40,48},{48,56},{56,64},{64,7... | collective-permute-start | bytes 394760 | tf_op jit(solution)/shard_map/ppermute | solution.py:18
  54.1 3.2 %collective-permute-start.4 = (bf16[32,1793]{1,0:T(8,128)(2,1)S(1)}, bf16[32,1793]{1,0:T(8,128)(2,1)S(1)}, u32[]{:S(2)}, u32[]{:S(2)}) collective-permute-start(bf16[32,1793]{1,0:T(8,128)(2,1)S(1)} %pad_maximum_fusion.1), channel_id=1, source_target_pairs={{0,8},{8,0},{16,24},{24,16},{32,40},{40,32},{48,56},{56,48},{64,72... | collective-permute-start | bytes 344264 | tf_op jit(solution)/shard_map/ppermute | solution.py:25
  57.6 7.3 %collective-permute-start.5 = (bf16[32,1793]{1,0:T(8,128)(2,1)S(1)}, bf16[32,1793]{1,0:T(8,128)(2,1)S(1)}, u32[]{:S(2)}, u32[]{:S(2)}) collective-permute-start(bf16[32,1793]{1,0:T(8,128)(2,1)S(1)} %broadcast_select_fusion.4), channel_id=1, source_target_pairs={{0,16},{8,24},{16,0},{24,8},{32,48},{40,56},{48,32},{56,40},{64,80... | collective-permute-start | bytes 344264 | tf_op jit(solution)/shard_map/ppermute | solution.py:25
  65.1 8.3 %collective-permute-start.6 = (bf16[32,1793]{1,0:T(8,128)(2,1)S(1)}, bf16[32,1793]{1,0:T(8,128)(2,1)S(1)}, u32[]{:S(2)}, u32[]{:S(2)}) collective-permute-start(bf16[32,1793]{1,0:T(8,128)(2,1)S(1)} %broadcast_select_fusion.3), channel_id=1, source_target_pairs={{0,32},{8,40},{16,48},{24,56},{32,0},{40,8},{48,16},{56,24},{64,96... | collective-permute-start | bytes 344264 | tf_op jit(solution)/shard_map/ppermute | solution.py:25
  73.6 9.8 %collective-permute-start.7 = (bf16[32,1793]{1,0:T(8,128)(2,1)S(1)}, bf16[32,1793]{1,0:T(8,128)(2,1)S(1)}, u32[]{:S(2)}, u32[]{:S(2)}) collective-permute-start(bf16[32,1793]{1,0:T(8,128)(2,1)S(1)} %broadcast_select_fusion.2), channel_id=1, source_target_pairs={{0,64},{8,72},{16,80},{24,88},{32,96},{40,104},{48,112},{56,120},{... | collective-permute-start | bytes 344264 | tf_op jit(solution)/shard_map/ppermute | solution.py:25
  83.6 15.1 %collective-permute-start.8 = (bf16[32,1793]{1,0:T(8,128)(2,1)S(1)}, bf16[32,1793]{1,0:T(8,128)(2,1)S(1)}, u32[]{:S(2)}, u32[]{:S(2)}) collective-permute-start(bf16[32,1793]{1,0:T(8,128)(2,1)S(1)} %broadcast_select_fusion.1), channel_id=1, source_target_pairs={{0,128},{8,136},{16,144},{24,152},{32,160},{40,168},{48,176},{56,1... | collective-permute-start | bytes 344264 | tf_op jit(solution)/shard_map/ppermute | solution.py:25
  98.9 14.7 %collective-permute-start.9 = (bf16[32,1793]{1,0:T(8,128)(2,1)S(1)}, bf16[32,1793]{1,0:T(8,128)(2,1)S(1)}, u32[]{:S(2)}, u32[]{:S(2)}) collective-permute-start(bf16[32,1793]{1,0:T(8,128)(2,1)S(1)} %broadcast_select_fusion), channel_id=1, source_target_pairs={{0,256},{8,264},{16,272},{24,280},{32,288},{40,296},{48,304},{56,3... | collective-permute-start | bytes 344264 | tf_op jit(solution)/shard_map/ppermute | solution.py:25
  122.5 41.9 %copy-start.2 = (bf16[896]{0:T(1024)(128)(2,1)S(1)}, bf16[896]{0:T(1024)(128)(2,1)}, u32[]{:S(2)}) copy-start(bf16[896]{0:T(1024)(128)(2,1)} %param.12) | copy-start | bytes 5380
  134.8 9.7 %collective-permute-start.10 = (bf16[32,4,896]{2,0,1:T(8,128)(2,1)S(1)}, bf16[32,4,896]{2,0,1:T(8,128)(2,1)S(1)}, u32[]{:S(2)}, u32[]{:S(2)}) collective-permute-start(bf16[32,4,896]{2,0,1:T(8,128)(2,1)S(1)} %dynamic-slice_bitcast_fusion), channel_id=1, source_target_pairs={{0,1},{1,0},{2,3},{3,2},{4,5},{5,4},{6,7},{7,6},{8,9},{9,8},{10,11... | collective-permute-start | bytes 688136 | tf_op jit(solution)/shard_map/ppermute | solution.py:42
  144.5 9.7 %collective-permute-start.11 = (bf16[32,2,896]{2,0,1:T(8,128)(2,1)S(1)}, bf16[32,2,896]{2,0,1:T(8,128)(2,1)S(1)}, u32[]{:S(2)}, u32[]{:S(2)}) collective-permute-start(bf16[32,2,896]{2,0,1:T(8,128)(2,1)S(1)} %dynamic-slice_bitcast_fusion.1), channel_id=1, source_target_pairs={{0,2},{1,3},{2,0},{3,1},{4,6},{5,7},{6,4},{7,5},{8,10},{9,11},{10,... | collective-permute-start | bytes 344072 | tf_op jit(solution)/shard_map/ppermute | solution.py:42
  154.3 10.0 %collective-permute-start.12 = (bf16[32,1,896]{2,0,1:T(8,128)(2,1)S(1)}, bf16[32,1,896]{2,0,1:T(8,128)(2,1)S(1)}, u32[]{:S(2)}, u32[]{:S(2)}) collective-permute-start(bf16[32,1,896]{2,0,1:T(8,128)(2,1)S(1)} %constant_dynamic-slice_fusion), channel_id=1, source_target_pairs={{0,4},{1,5},{2,6},{3,7},{4,0},{5,1},{6,2},{7,3},{8,12},{9,13},{10,... | collective-permute-start | bytes 172040 | tf_op jit(solution)/shard_map/ppermute | solution.py:42
  165.3 6.2 %collective-permute-start.13 = (bf16[32,1001]{1,0:T(8,128)(2,1)S(1)}, bf16[32,1001]{1,0:T(8,128)(2,1)S(1)}, u32[]{:S(2)}, u32[]{:S(2)}) collective-permute-start(bf16[32,1001]{1,0:T(8,128)(2,1)S(1)} %pad_maximum_fusion.3), channel_id=1, source_target_pairs={{0,1},{1,0},{2,3},{3,2},{4,5},{5,4},{6,7},{7,6},{8,9},{9,8},{10,11... | collective-permute-start | bytes 192200 | tf_op jit(solution)/shard_map/ppermute | solution.py:25
  171.6 8.2 %collective-permute-start.14 = (bf16[32,1001]{1,0:T(8,128)(2,1)S(1)}, bf16[32,1001]{1,0:T(8,128)(2,1)S(1)}, u32[]{:S(2)}, u32[]{:S(2)}) collective-permute-start(bf16[32,1001]{1,0:T(8,128)(2,1)S(1)} %fusion.64), channel_id=1, source_target_pairs={{0,2},{1,3},{2,0},{3,1},{4,6},{5,7},{6,4},{7,5},{8,10},{9,11},{10,... | collective-permute-start | bytes 192200 | tf_op jit(solution)/shard_map/ppermute | solution.py:25
  179.8 12.0 %collective-permute-start.15 = (bf16[32,1001]{1,0:T(8,128)(2,1)S(1)}, bf16[32,1001]{1,0:T(8,128)(2,1)S(1)}, u32[]{:S(2)}, u32[]{:S(2)}) collective-permute-start(bf16[32,1001]{1,0:T(8,128)(2,1)S(1)} %add.116), channel_id=1, source_target_pairs={{0,4},{1,5},{2,6},{3,7},{4,0},{5,1},{6,2},{7,3},{8,12},{9,13},{10,... | collective-permute-start | bytes 192200 | tf_op jit(solution)/shard_map/ppermute | solution.py:25
  192.8 3.0 %collective-permute-start.16 = (f32[32]{0:T(128)S(1)}, f32[32]{0:T(128)S(1)}, u32[]{:S(2)}, u32[]{:S(2)}) collective-permute-start(f32[32]{0:T(128)S(1)} %fusion.41), channel_id=1, source_target_pairs={{0,8},{8,0},{16,24},{24,16},{32,40},{40,32},{48,56},{56,48},{64,72... | collective-permute-start | bytes 392 | tf_op jit(solution)/shard_map/ppermute | solution.py:25
  195.8 5.4 %collective-permute-start.17 = (f32[32]{0:T(128)S(1)}, f32[32]{0:T(128)S(1)}, u32[]{:S(2)}, u32[]{:S(2)}) collective-permute-start(f32[32]{0:T(128)S(1)} %max.18), channel_id=1, source_target_pairs={{0,16},{8,24},{16,0},{24,8},{32,48},{40,56},{48,32},{56,40},{64,80... | collective-permute-start | bytes 392 | tf_op jit(solution)/shard_map/ppermute | solution.py:25
  201.2 6.9 %collective-permute-start.18 = (f32[32]{0:T(128)S(1)}, f32[32]{0:T(128)S(1)}, u32[]{:S(2)}, u32[]{:S(2)}) collective-permute-start(f32[32]{0:T(128)S(1)} %max.19), channel_id=1, source_target_pairs={{0,32},{8,40},{16,48},{24,56},{32,0},{40,8},{48,16},{56,24},{64,96... | collective-permute-start | bytes 392 | tf_op jit(solution)/shard_map/ppermute | solution.py:25
  208.1 5.4 %collective-permute-start.19 = (f32[32]{0:T(128)S(1)}, f32[32]{0:T(128)S(1)}, u32[]{:S(2)}, u32[]{:S(2)}) collective-permute-start(f32[32]{0:T(128)S(1)} %max.20), channel_id=1, source_target_pairs={{0,64},{8,72},{16,80},{24,88},{32,96},{40,104},{48,112},{56,120},{... | collective-permute-start | bytes 392 | tf_op jit(solution)/shard_map/ppermute | solution.py:25
  213.6 6.3 %collective-permute-start.20 = (f32[32]{0:T(128)S(1)}, f32[32]{0:T(128)S(1)}, u32[]{:S(2)}, u32[]{:S(2)}) collective-permute-start(f32[32]{0:T(128)S(1)} %max.21), channel_id=1, source_target_pairs={{0,128},{8,136},{16,144},{24,152},{32,160},{40,168},{48,176},{56,1... | collective-permute-start | bytes 392 | tf_op jit(solution)/shard_map/ppermute | solution.py:25
  219.9 9.3 %collective-permute-start.21 = (f32[32]{0:T(128)S(1)}, f32[32]{0:T(128)S(1)}, u32[]{:S(2)}, u32[]{:S(2)}) collective-permute-start(f32[32]{0:T(128)S(1)} %max.22), channel_id=1, source_target_pairs={{0,256},{8,264},{16,272},{24,280},{32,288},{40,296},{48,304},{56,3... | collective-permute-start | bytes 392 | tf_op jit(solution)/shard_map/ppermute | solution.py:25
Sparse Core Ops, SparseCore 0:
  11.3 111.1 all-gather.1
  164.5 56.8 reduce-scatter.1
where the time goes:
time: 240 us; the launch traced here: 239 us
  waiting for transfers between devices  93.8 us (39%)
  starting transfers between devices  79.9 us (33%)
  other arithmetic  20.6 us (9%)
  matrix products  17.5 us (7%)
  between operations  14.6 us (6%)
  local copies, waits for them, and re-layouts  12.2 us (5%)
    ppermute x15, waiting for transfers between devices, butterfly(): lax.ppermute(value, axis, [(source, source ^ stride) for source in range(...  67.4 us
    ppermute x15, starting transfers between devices, butterfly(): lax.ppermute(value, axis, [(source, source ^ stride) for source in range(...  53 us
    ppermute x3, waiting for transfers between devices, halving_scatter(): lax.ppermute(give, axis, [(source, source ^ bit) for source in range(coun...  18 us
    ppermute x4, starting transfers between devices, from_behind(): lax.ppermute(value, axis, [(source, source + steps) for source in range(i...  15.6 us
    ppermute x3, starting transfers between devices, halving_scatter(): lax.ppermute(give, axis, [(source, source ^ bit) for source in range(coun...  11.2 us
    dot_general x1, matrix products, local(): jnp.einsum('tk,kgn->gtn', jnp.concatenate([attended, end_att], axis=0), f...  11.2 us
    all_gather x1, waiting for transfers between devices, local(): full_weight = lax.all_gather(out_weight, 'req', axis=1, tiled=True)  7.7 us
  transfers between devices with their start and end apart: 24, of which 19 were waited for; matrix products, arithmetic and copies ran while one was open for 15% of the time, Pallas kernels for 0%

commit v1 on v0

--- a/solution.py
+++ b/solution.py
@@ -154,7 +154,9 @@
     end_rows = butterfly(end_rows, "req", latest)[:, :-1]
     attended, end_rows = lax.optimization_barrier((attended, end_rows))
     end_att, end_res = (end_rows[:, : attended.shape[1]], end_rows[:, attended.shape[1] :])
-    full_weight = lax.all_gather(out_weight, "req", axis=1, tiled=True)
+    full_weight = jnp.concatenate(
+        lax.all_to_all(jnp.stack([out_weight] * lax.axis_size("req")), "req", 0, 0), axis=1
+    )
     groups = lax.axis_size("tp")
     both = jnp.einsum(
         "tk,kgn->gtn",

time: 240 us -> 505 us (2.10)
  starting transfers between devices: 79.9 us -> 335 us
  waiting for transfers between devices: 93.8 us -> 99.5 us
    ppermute x15, starting transfers between devices: 53 us -> 294 us  [butterfly(): lax.ppermute(value, axis, [(source, source ^ stride) for source in range(...]
    ppermute x4, waiting for transfers between devices: 0.01 us -> 31.8 us  [from_behind(): lax.ppermute(value, axis, [(source, source + steps) for source in range(i...]
    ppermute x15, waiting for transfers between devices: 67.4 us -> 52.2 us  [butterfly(): lax.ppermute(value, axis, [(source, source ^ stride) for source in range(...]
    all_to_all x0 -> x1, starting transfers between devices: none -> 14.1 us  [local(): lax.all_to_all(jnp.stack([out_weight] * lax.axis_size('req')), 'req', 0, 0)]
    all_gather x1 -> x0, waiting for transfers between devices: 7.7 us -> none  [local(): full_weight = lax.all_gather(out_weight, 'req', axis=1, tiled=True)]
    another operation x0 -> x1, local copies, waits for them, and re-layouts: none -> 6.6 us  [local(): jnp.stack([out_weight] * lax.axis_size('req'))]
  transfers between devices with their start and end apart: 24 -> 24, of which waited for: 19 -> 21; matrix products, arithmetic and copies ran while one was open for 15% -> 6% of each run, Pallas kernels for 0% -> 0%
where the time goes in v1:
time: 505 us; the launch traced here: 502 us
  starting transfers between devices  335 us (66%)
  waiting for transfers between devices  99.5 us (20%)
  other arithmetic  18.2 us (4%)
  matrix products  17.5 us (3%)
  local copies, waits for them, and re-layouts  17.1 us (3%)
  between operations  14.6 us (3%)
    ppermute x15, starting transfers between devices, butterfly(): lax.ppermute(value, axis, [(source, source ^ stride) for source in range(...  294 us
    ppermute x15, waiting for transfers between devices, butterfly(): lax.ppermute(value, axis, [(source, source ^ stride) for source in range(...  52.2 us
    ppermute x4, waiting for transfers between devices, from_behind(): lax.ppermute(value, axis, [(source, source + steps) for source in range(i...  31.8 us
    ppermute x3, waiting for transfers between devices, halving_scatter(): lax.ppermute(give, axis, [(source, source ^ bit) for source in range(coun...  15.5 us
    ppermute x4, starting transfers between devices, from_behind(): lax.ppermute(value, axis, [(source, source + steps) for source in range(i...  14.7 us
    all_to_all x1, starting transfers between devices, local(): lax.all_to_all(jnp.stack([out_weight] * lax.axis_size('req')), 'req', 0, 0)  14.1 us
    ppermute x3, starting transfers between devices, halving_scatter(): lax.ppermute(give, axis, [(source, source ^ bit) for source in range(coun...  11.9 us
    dot_general x1, matrix products, local(): jnp.einsum('tk,kgn->gtn', jnp.concatenate([attended, end_att], axis=0), f...  11.2 us
  transfers between devices with their start and end apart: 24, of which 21 were waited for; matrix products, arithmetic and copies ran while one was open for 6% of the time, Pallas kernels for 0%

profile of v1, /device:TPU:56, one launch (start us, length us, event | category | flops | bytes accessed | tf_op | source)
XLA Modules:
  0.0 502.0 jit_solution(5473272313386717117)
XLA Ops:
  7.2 6.6 %stack.2 = bf16[64,896,112]{1,2,0:T(8,128)(2,1)} broadcast(bf16[896,112]{0,1:T(8,128)(2,1)} %param.11), dimensions={1,2} | broadcast | bytes 13045760 | tf_op jit(solution)/shard_map/stack | solution.py:158
  13.8 14.1 %all-to-all-start = ((bf16[64,896,112]{1,2,0:T(8,128)(2,1)}), bf16[64,896,112]{1,2,0:T(8,128)(2,1)}, u32[]{:S(2)}, u32[]{:S(2)}) async-start(bf16[64,896,112]{1,2,0:T(8,128)(2,1)} %stack.2), calls=%async_computation | async-start | bytes 25690112 | tf_op jit(solution)/shard_map/all_to_all | solution.py:158
  28.0 5.6 %collective-permute-start = (bf16[514,128]{1,0:T(8,128)(2,1)S(1)}, bf16[514,128]{1,0:T(8,128)(2,1)}, u32[]{:S(2)}, u32[]{:S(2)}) collective-permute-start(bf16[514,128]{1,0:T(8,128)(2,1)S(1)} %pad_maximum_fusion), channel_id=1, source_target_pairs={{0,32},{8,40},{16,48},{24,56},{32,64},{40,72},{48,80},{56,88},{64,... | collective-permute-start | bytes 394760 | tf_op jit(solution)/shard_map/ppermute | solution.py:18
  39.0 3.8 collective-permute-start.3
  46.9 18.1 %collective-permute-done = bf16[514,128]{1,0:T(8,128)(2,1)} collective-permute-done((bf16[514,128]{1,0:T(8,128)(2,1)S(1)}, bf16[514,128]{1,0:T(8,128)(2,1)}, u32[]{:S(2)}, u32[]{:S(2)}) %collective-permute-start) | collective-permute-done | bytes 131616 | tf_op jit(solution)/shard_map/ppermute | solution.py:18
  65.9 10.9 %collective-permute-done.1 = bf16[514,128]{1,0:T(8,128)(2,1)} collective-permute-done((bf16[514,128]{1,0:T(8,128)(2,1)S(1)}, bf16[514,128]{1,0:T(8,128)(2,1)}, u32[]{:S(2)}, u32[]{:S(2)}) %collective-permute-start.1) | collective-permute-done | bytes 131616 | tf_op jit(solution)/shard_map/ppermute | solution.py:18
  90.2 3.0 fusion.25
  104.5 4.5 collective-permute-start.5
  109.0 5.8 %collective-permute-done.5 = bf16[32,1793]{1,0:T(8,128)(2,1)S(1)} collective-permute-done((bf16[32,1793]{1,0:T(8,128)(2,1)S(1)}, bf16[32,1793]{1,0:T(8,128)(2,1)S(1)}, u32[]{:S(2)}, u32[]{:S(2)}) %collective-permute-start.5) | collective-permute-done | bytes 114784 | tf_op jit(solution)/shard_map/ppermute | solution.py:25
  115.0 235.8 %collective-permute-start.6 = (bf16[32,1793]{1,0:T(8,128)(2,1)S(1)}, bf16[32,1793]{1,0:T(8,128)(2,1)S(1)}, u32[]{:S(2)}, u32[]{:S(2)}) collective-permute-start(bf16[32,1793]{1,0:T(8,128)(2,1)S(1)} %broadcast_select_fusion.3), channel_id=1, source_target_pairs={{0,32},{8,40},{16,48},{24,56},{32,0},{40,8},{48,16},{56,24},{64,96... | collective-permute-start | bytes 344264 | tf_op jit(solution)/shard_map/ppermute | solution.py:25
  350.8 3.1 collective-permute-done.6
  354.2 7.5 %collective-permute-start.7 = (bf16[32,1793]{1,0:T(8,128)(2,1)S(1)}, bf16[32,1793]{1,0:T(8,128)(2,1)S(1)}, u32[]{:S(2)}, u32[]{:S(2)}) collective-permute-start(bf16[32,1793]{1,0:T(8,128)(2,1)S(1)} %broadcast_select_fusion.2), channel_id=1, source_target_pairs={{0,64},{8,72},{16,80},{24,88},{32,96},{40,104},{48,112},{56,120},{... | collective-permute-start | bytes 344264 | tf_op jit(solution)/shard_map/ppermute | solution.py:25
  364.7 5.3 %collective-permute-start.8 = (bf16[32,1793]{1,0:T(8,128)(2,1)S(1)}, bf16[32,1793]{1,0:T(8,128)(2,1)S(1)}, u32[]{:S(2)}, u32[]{:S(2)}) collective-permute-start(bf16[32,1793]{1,0:T(8,128)(2,1)S(1)} %broadcast_select_fusion.1), channel_id=1, source_target_pairs={{0,128},{8,136},{16,144},{24,152},{32,160},{40,168},{48,176},{56,1... | collective-permute-start | bytes 344264 | tf_op jit(solution)/shard_map/ppermute | solution.py:25
  373.0 6.2 %collective-permute-start.9 = (bf16[32,1793]{1,0:T(8,128)(2,1)S(1)}, bf16[32,1793]{1,0:T(8,128)(2,1)S(1)}, u32[]{:S(2)}, u32[]{:S(2)}) collective-permute-start(bf16[32,1793]{1,0:T(8,128)(2,1)S(1)} %broadcast_select_fusion), channel_id=1, source_target_pairs={{0,256},{8,264},{16,272},{24,280},{32,288},{40,296},{48,304},{56,3... | collective-permute-start | bytes 344264 | tf_op jit(solution)/shard_map/ppermute | solution.py:25
  379.3 5.0 %collective-permute-done.9 = bf16[32,1793]{1,0:T(8,128)(2,1)S(1)} collective-permute-done((bf16[32,1793]{1,0:T(8,128)(2,1)S(1)}, bf16[32,1793]{1,0:T(8,128)(2,1)S(1)}, u32[]{:S(2)}, u32[]{:S(2)}) %collective-permute-start.9) | collective-permute-done | bytes 114784 | tf_op jit(solution)/shard_map/ppermute | solution.py:25
  385.6 11.2 %convert_bitcast_fusion = bf16[8,288,896]{2,1,0:T(8,128)(2,1)} fusion(bf16[896,8,896]{0,2,1:T(8,128)(2,1)} %bitcast.33, bf16[32,896]{1,0:T(8,128)(2,1)S(1)} %slice.145, bf16[256,896]{1,0:T(8,128)(2,1)} %copy.40), kind=kOutput, calls=%fused_computation.9 | convolution fusion | flops 3702472704 | bytes 17489920 | tf_op jit(solution)/shard_map/tk,kgn->gtn/dot_general | solution.py:161
  397.9 3.2 collective-permute-start.10
  401.2 4.6 collective-permute-done.10
  405.9 4.6 collective-permute-start.11
  410.5 4.8 collective-permute-done.11
  415.4 4.1 collective-permute-start.12
  419.5 6.0 %collective-permute-done.12 = bf16[32,1,896]{2,0,1:T(8,128)(2,1)S(1)} collective-permute-done((bf16[32,1,896]{2,0,1:T(8,128)(2,1)S(1)}, bf16[32,1,896]{2,0,1:T(8,128)(2,1)S(1)}, u32[]{:S(2)}, u32[]{:S(2)}) %collective-permute-start.12) | collective-permute-done | bytes 57376 | tf_op jit(solution)/shard_map/ppermute | solution.py:42
  428.6 4.1 collective-permute-done.13
  432.7 3.2 collective-permute-start.14
  436.0 4.6 collective-permute-done.14
  440.6 5.1 %collective-permute-start.15 = (bf16[32,1001]{1,0:T(8,128)(2,1)S(1)}, bf16[32,1001]{1,0:T(8,128)(2,1)S(1)}, u32[]{:S(2)}, u32[]{:S(2)}) collective-permute-start(bf16[32,1001]{1,0:T(8,128)(2,1)S(1)} %add.116), channel_id=1, source_target_pairs={{0,4},{1,5},{2,6},{3,7},{4,0},{5,1},{6,2},{7,3},{8,12},{9,13},{10,... | collective-permute-start | bytes 192200 | tf_op jit(solution)/shard_map/ppermute | solution.py:25
  445.7 6.8 %collective-permute-done.15 = bf16[32,1001]{1,0:T(8,128)(2,1)S(1)} collective-permute-done((bf16[32,1001]{1,0:T(8,128)(2,1)S(1)}, bf16[32,1001]{1,0:T(8,128)(2,1)S(1)}, u32[]{:S(2)}, u32[]{:S(2)}) %collective-permute-start.15) | collective-permute-done | bytes 64096 | tf_op jit(solution)/shard_map/ppermute | solution.py:25
  464.2 4.6 collective-permute-done.18
  468.8 3.6 collective-permute-start.19
  474.2 7.5 %collective-permute-start.20 = (f32[32]{0:T(128)S(1)}, f32[32]{0:T(128)S(1)}, u32[]{:S(2)}, u32[]{:S(2)}) collective-permute-start(f32[32]{0:T(128)S(1)} %max.21), channel_id=1, source_target_pairs={{0,128},{8,136},{16,144},{24,152},{32,160},{40,168},{48,176},{56,1... | collective-permute-start | bytes 392 | tf_op jit(solution)/shard_map/ppermute | solution.py:25
  483.3 4.4 collective-permute-start.21
  488.4 4.2 collective-permute-done.21
  (112 shorter events, 65.2 us)
Async XLA Ops:
  7.2 418.6 %copy-start = (bf16[896,1000]{0,1:T(8,128)(2,1)S(1)}, bf16[896,1000]{0,1:T(8,128)(2,1)}, u32[]{:S(2)}) copy-start(bf16[896,1000]{0,1:T(8,128)(2,1)} %param.13) | copy-start | bytes 5376004
  13.8 14.2 %copy-start.3 = (s32[256]{0:T(256)S(1)}, s32[256]{0:T(256)}, u32[]{:S(2)}) copy-start(s32[256]{0:T(256)} %param.9) | copy-start | bytes 3076
  13.8 14.2 %copy-start.1 = (bf16[2,256,128]{2,1,0:T(8,128)(2,1)S(1)}, bf16[2,256,128]{2,1,0:T(8,128)(2,1)}, u32[]{:S(2)}) copy-start(bf16[2,256,128]{2,1,0:T(8,128)(2,1)} %param.8) | copy-start | bytes 393220
  13.8 29.0 %copy-start.2 = (bf16[256,896]{1,0:T(8,128)(2,1)S(1)}, bf16[256,896]{1,0:T(8,128)(2,1)}, u32[]{:S(2)}) copy-start(bf16[256,896]{1,0:T(8,128)(2,1)} %param.7) | copy-start | bytes 1376260
  13.8 371.8 %all-to-all-start = ((bf16[64,896,112]{1,2,0:T(8,128)(2,1)}), bf16[64,896,112]{1,2,0:T(8,128)(2,1)}, u32[]{:S(2)}, u32[]{:S(2)}) async-start(bf16[64,896,112]{1,2,0:T(8,128)(2,1)} %stack.2), calls=%async_computation | async-start | bytes 25690112 | tf_op jit(solution)/shard_map/all_to_all | solution.py:158
  27.9 465.2 %reduce-scatter.2.cloned.1.call-start = ((), (), s32[]{:S(2)}) async-start(), calls=%async_computation.2 | async-start | bytes 4644864 | tf_op jit(solution)/shard_map/reduce_scatter | solution.py:170
  28.0 36.9 %collective-permute-start = (bf16[514,128]{1,0:T(8,128)(2,1)S(1)}, bf16[514,128]{1,0:T(8,128)(2,1)}, u32[]{:S(2)}, u32[]{:S(2)}) collective-permute-start(bf16[514,128]{1,0:T(8,128)(2,1)S(1)} %pad_maximum_fusion), channel_id=1, source_target_pairs={{0,32},{8,40},{16,48},{24,56},{32,64},{40,72},{48,80},{56,88},{64,... | collective-permute-start | bytes 394760 | tf_op jit(solution)/shard_map/ppermute | solution.py:18
  33.6 43.2 %collective-permute-start.1 = (bf16[514,128]{1,0:T(8,128)(2,1)S(1)}, bf16[514,128]{1,0:T(8,128)(2,1)}, u32[]{:S(2)}, u32[]{:S(2)}) collective-permute-start(bf16[514,128]{1,0:T(8,128)(2,1)S(1)} %pad_maximum_fusion), channel_id=1, source_target_pairs={{0,24},{8,32},{16,40},{24,48},{32,56},{40,64},{48,72},{56,80},{64,... | collective-permute-start | bytes 394760 | tf_op jit(solution)/shard_map/ppermute | solution.py:18
  36.2 44.3 %collective-permute-start.2 = (bf16[514,128]{1,0:T(8,128)(2,1)S(1)}, bf16[514,128]{1,0:T(8,128)(2,1)}, u32[]{:S(2)}, u32[]{:S(2)}) collective-permute-start(bf16[514,128]{1,0:T(8,128)(2,1)S(1)} %pad_maximum_fusion), channel_id=1, source_target_pairs={{0,16},{8,24},{16,32},{24,40},{32,48},{40,56},{48,64},{56,72},{64,... | collective-permute-start | bytes 394760 | tf_op jit(solution)/shard_map/ppermute | solution.py:18
  39.0 42.5 %collective-permute-start.3 = (bf16[514,128]{1,0:T(8,128)(2,1)S(1)}, bf16[514,128]{1,0:T(8,128)(2,1)}, u32[]{:S(2)}, u32[]{:S(2)}) collective-permute-start(bf16[514,128]{1,0:T(8,128)(2,1)S(1)} %pad_maximum_fusion), channel_id=1, source_target_pairs={{0,8},{8,16},{16,24},{24,32},{32,40},{40,48},{48,56},{56,64},{64,7... | collective-permute-start | bytes 394760 | tf_op jit(solution)/shard_map/ppermute | solution.py:18
  101.0 3.2 collective-permute-start.4
  104.5 10.3 %collective-permute-start.5 = (bf16[32,1793]{1,0:T(8,128)(2,1)S(1)}, bf16[32,1793]{1,0:T(8,128)(2,1)S(1)}, u32[]{:S(2)}, u32[]{:S(2)}) collective-permute-start(bf16[32,1793]{1,0:T(8,128)(2,1)S(1)} %broadcast_select_fusion.4), channel_id=1, source_target_pairs={{0,16},{8,24},{16,0},{24,8},{32,48},{40,56},{48,32},{56,40},{64,80... | collective-permute-start | bytes 344264 | tf_op jit(solution)/shard_map/ppermute | solution.py:25
  115.0 239.0 %collective-permute-start.6 = (bf16[32,1793]{1,0:T(8,128)(2,1)S(1)}, bf16[32,1793]{1,0:T(8,128)(2,1)S(1)}, u32[]{:S(2)}, u32[]{:S(2)}) collective-permute-start(bf16[32,1793]{1,0:T(8,128)(2,1)S(1)} %broadcast_select_fusion.3), channel_id=1, source_target_pairs={{0,32},{8,40},{16,48},{24,56},{32,0},{40,8},{48,16},{56,24},{64,96... | collective-permute-start | bytes 344264 | tf_op jit(solution)/shard_map/ppermute | solution.py:25
  354.2 10.3 %collective-permute-start.7 = (bf16[32,1793]{1,0:T(8,128)(2,1)S(1)}, bf16[32,1793]{1,0:T(8,128)(2,1)S(1)}, u32[]{:S(2)}, u32[]{:S(2)}) collective-permute-start(bf16[32,1793]{1,0:T(8,128)(2,1)S(1)} %broadcast_select_fusion.2), channel_id=1, source_target_pairs={{0,64},{8,72},{16,80},{24,88},{32,96},{40,104},{48,112},{56,120},{... | collective-permute-start | bytes 344264 | tf_op jit(solution)/shard_map/ppermute | solution.py:25
  364.7 8.1 %collective-permute-start.8 = (bf16[32,1793]{1,0:T(8,128)(2,1)S(1)}, bf16[32,1793]{1,0:T(8,128)(2,1)S(1)}, u32[]{:S(2)}, u32[]{:S(2)}) collective-permute-start(bf16[32,1793]{1,0:T(8,128)(2,1)S(1)} %broadcast_select_fusion.1), channel_id=1, source_target_pairs={{0,128},{8,136},{16,144},{24,152},{32,160},{40,168},{48,176},{56,1... | collective-permute-start | bytes 344264 | tf_op jit(solution)/shard_map/ppermute | solution.py:25
  373.0 11.3 %collective-permute-start.9 = (bf16[32,1793]{1,0:T(8,128)(2,1)S(1)}, bf16[32,1793]{1,0:T(8,128)(2,1)S(1)}, u32[]{:S(2)}, u32[]{:S(2)}) collective-permute-start(bf16[32,1793]{1,0:T(8,128)(2,1)S(1)} %broadcast_select_fusion), channel_id=1, source_target_pairs={{0,256},{8,264},{16,272},{24,280},{32,288},{40,296},{48,304},{56,3... | collective-permute-start | bytes 344264 | tf_op jit(solution)/shard_map/ppermute | solution.py:25
  385.6 40.0 %copy-start.4 = (bf16[896]{0:T(1024)(128)(2,1)S(1)}, bf16[896]{0:T(1024)(128)(2,1)}, u32[]{:S(2)}) copy-start(bf16[896]{0:T(1024)(128)(2,1)} %param.12) | copy-start | bytes 5380
  397.9 7.9 %collective-permute-start.10 = (bf16[32,4,896]{2,0,1:T(8,128)(2,1)S(1)}, bf16[32,4,896]{2,0,1:T(8,128)(2,1)S(1)}, u32[]{:S(2)}, u32[]{:S(2)}) collective-permute-start(bf16[32,4,896]{2,0,1:T(8,128)(2,1)S(1)} %dynamic-slice_bitcast_fusion), channel_id=1, source_target_pairs={{0,1},{1,0},{2,3},{3,2},{4,5},{5,4},{6,7},{7,6},{8,9},{9,8},{10,11... | collective-permute-start | bytes 688136 | tf_op jit(solution)/shard_map/ppermute | solution.py:42
  405.9 9.4 %collective-permute-start.11 = (bf16[32,2,896]{2,0,1:T(8,128)(2,1)S(1)}, bf16[32,2,896]{2,0,1:T(8,128)(2,1)S(1)}, u32[]{:S(2)}, u32[]{:S(2)}) collective-permute-start(bf16[32,2,896]{2,0,1:T(8,128)(2,1)S(1)} %dynamic-slice_bitcast_fusion.1), channel_id=1, source_target_pairs={{0,2},{1,3},{2,0},{3,1},{4,6},{5,7},{6,4},{7,5},{8,10},{9,11},{10,... | collective-permute-start | bytes 344072 | tf_op jit(solution)/shard_map/ppermute | solution.py:42
  415.4 10.1 %collective-permute-start.12 = (bf16[32,1,896]{2,0,1:T(8,128)(2,1)S(1)}, bf16[32,1,896]{2,0,1:T(8,128)(2,1)S(1)}, u32[]{:S(2)}, u32[]{:S(2)}) collective-permute-start(bf16[32,1,896]{2,0,1:T(8,128)(2,1)S(1)} %constant_dynamic-slice_fusion), channel_id=1, source_target_pairs={{0,4},{1,5},{2,6},{3,7},{4,0},{5,1},{6,2},{7,3},{8,12},{9,13},{10,... | collective-permute-start | bytes 172040 | tf_op jit(solution)/shard_map/ppermute | solution.py:42
  426.5 6.2 %collective-permute-start.13 = (bf16[32,1001]{1,0:T(8,128)(2,1)S(1)}, bf16[32,1001]{1,0:T(8,128)(2,1)S(1)}, u32[]{:S(2)}, u32[]{:S(2)}) collective-permute-start(bf16[32,1001]{1,0:T(8,128)(2,1)S(1)} %pad_maximum_fusion.3), channel_id=1, source_target_pairs={{0,1},{1,0},{2,3},{3,2},{4,5},{5,4},{6,7},{7,6},{8,9},{9,8},{10,11... | collective-permute-start | bytes 192200 | tf_op jit(solution)/shard_map/ppermute | solution.py:25
  432.7 7.8 %collective-permute-start.14 = (bf16[32,1001]{1,0:T(8,128)(2,1)S(1)}, bf16[32,1001]{1,0:T(8,128)(2,1)S(1)}, u32[]{:S(2)}, u32[]{:S(2)}) collective-permute-start(bf16[32,1001]{1,0:T(8,128)(2,1)S(1)} %fusion.64), channel_id=1, source_target_pairs={{0,2},{1,3},{2,0},{3,1},{4,6},{5,7},{6,4},{7,5},{8,10},{9,11},{10,... | collective-permute-start | bytes 192200 | tf_op jit(solution)/shard_map/ppermute | solution.py:25
  440.6 11.9 %collective-permute-start.15 = (bf16[32,1001]{1,0:T(8,128)(2,1)S(1)}, bf16[32,1001]{1,0:T(8,128)(2,1)S(1)}, u32[]{:S(2)}, u32[]{:S(2)}) collective-permute-start(bf16[32,1001]{1,0:T(8,128)(2,1)S(1)} %add.116), channel_id=1, source_target_pairs={{0,4},{1,5},{2,6},{3,7},{4,0},{5,1},{6,2},{7,3},{8,12},{9,13},{10,... | collective-permute-start | bytes 192200 | tf_op jit(solution)/shard_map/ppermute | solution.py:25
  453.4 3.0 collective-permute-start.16
  456.4 5.4 %collective-permute-start.17 = (f32[32]{0:T(128)S(1)}, f32[32]{0:T(128)S(1)}, u32[]{:S(2)}, u32[]{:S(2)}) collective-permute-start(f32[32]{0:T(128)S(1)} %max.18), channel_id=1, source_target_pairs={{0,16},{8,24},{16,0},{24,8},{32,48},{40,56},{48,32},{56,40},{64,80... | collective-permute-start | bytes 392 | tf_op jit(solution)/shard_map/ppermute | solution.py:25
  461.9 6.9 %collective-permute-start.18 = (f32[32]{0:T(128)S(1)}, f32[32]{0:T(128)S(1)}, u32[]{:S(2)}, u32[]{:S(2)}) collective-permute-start(f32[32]{0:T(128)S(1)} %max.19), channel_id=1, source_target_pairs={{0,32},{8,40},{16,48},{24,56},{32,0},{40,8},{48,16},{56,24},{64,96... | collective-permute-start | bytes 392 | tf_op jit(solution)/shard_map/ppermute | solution.py:25
  468.8 5.4 %collective-permute-start.19 = (f32[32]{0:T(128)S(1)}, f32[32]{0:T(128)S(1)}, u32[]{:S(2)}, u32[]{:S(2)}) collective-permute-start(f32[32]{0:T(128)S(1)} %max.20), channel_id=1, source_target_pairs={{0,64},{8,72},{16,80},{24,88},{32,96},{40,104},{48,112},{56,120},{... | collective-permute-start | bytes 392 | tf_op jit(solution)/shard_map/ppermute | solution.py:25
  474.2 9.1 %collective-permute-start.20 = (f32[32]{0:T(128)S(1)}, f32[32]{0:T(128)S(1)}, u32[]{:S(2)}, u32[]{:S(2)}) collective-permute-start(f32[32]{0:T(128)S(1)} %max.21), channel_id=1, source_target_pairs={{0,128},{8,136},{16,144},{24,152},{32,160},{40,168},{48,176},{56,1... | collective-permute-start | bytes 392 | tf_op jit(solution)/shard_map/ppermute | solution.py:25
  483.3 9.3 %collective-permute-start.21 = (f32[32]{0:T(128)S(1)}, f32[32]{0:T(128)S(1)}, u32[]{:S(2)}, u32[]{:S(2)}) collective-permute-start(f32[32]{0:T(128)S(1)} %max.22), channel_id=1, source_target_pairs={{0,256},{8,264},{16,272},{24,280},{32,288},{40,296},{48,304},{56,3... | collective-permute-start | bytes 392 | tf_op jit(solution)/shard_map/ppermute | solution.py:25
Sparse Core Ops, SparseCore 0:
  425.6 56.7 reduce-scatter.1
